TPU v7x, 128 devices: a whole 4x4x4 slice. The times are simulated.
128 devices in a mesh: req: 8 (over z, core), shard: 16 (over x, y).
Axes of the slice: x: 4, y: 4, z: 4, core: 2. Of those that a mesh axis runs over, the one named last changes fastest.
Arguments:
- hidden_states: bfloat16 [16384, 1536], P(('req', 'shard')), may hold values from -6 to 6
- attn_gain: float32 [1536], replicated, may hold values from 0.5 to 1.5
- w_qkv: bfloat16 [1536, 2560], replicated, may hold values from -0.15625 to 0.15625
- w_out: bfloat16 [1536, 1536], replicated, may hold values from -0.15625 to 0.15625
- kv_cache: bfloat16 [8, 4096, 1024], P('req', 'shard'), may hold values from -80 to 80, as said below
- cached_len: int32 [8], P('req'), may hold values from 128 to 4096, as said below
- ffn_gain: float32 [1536], replicated, may hold values from 0.5 to 1.5
- w_router: bfloat16 [1536, 40], replicated, may hold values from -0.15625 to 0.15625
- expert_ids: int32 [16384, 8], P(('req', 'shard')), may hold values from 0 to 39, all different within a row; in each aligned block of 128 rows (0 to 127, 128 to 255, ...) at most 32 rows name the same one
- w_gate: bfloat16 [40, 512, 1536], P('req', 'shard'), may hold values from -0.15625 to 0.15625
- w_up: bfloat16 [40, 512, 1536], P('req', 'shard'), may hold values from -0.15625 to 0.15625
- w_down: bfloat16 [40, 512, 1536], P('req', 'shard'), may hold values from -0.25 to 0.25
Outputs:
- layer_out: bfloat16 [16384, 1536], P(('req', 'shard'))
Inputs may be any that keep to these rules, and one draw needn't show every extreme that they name: `cached_len`: each request's length is drawn either between 128 and 512 or between 3072 and 4096; some request has exactly 4096. `expert_ids`: among the 128 rows of one device no expert is named by more than 32 rows. `kv_cache`: cached keys and values, already rotated.
All inputs are finite; a program needn't handle non-finite values.
Results may differ from a plain program's by a relative error of at most 0.025.
Values may be sent and summed in bfloat16 or wider, within the bound.
No kernel may reach another device: no remote copies, remote signals or barrier semaphores. Data moves between devices by JAX's collectives and lax.ppermute only.
A program may use at most 192 MiB of HBM per device.

v0:
```python
import functools
import math

import jax
import jax.numpy as jnp
from jax import lax
from jax.experimental import pallas as pl
from jax.experimental.pallas import tpu as pltpu
from jax.sharding import PartitionSpec as P

D = 1536
HEADS = 24
KVH = 8
HD = 64
TOP = 8


EPSILON = 1e-05
NEG_FILL = -1e30
FAR_LIMIT = 1 << 30
BLK = 512
NEG = NEG_FILL

def attn_kernel(meta_ref, q_ref, cache_ref, new_ref, o_ref, m_sc, l_sc, acc_sc, *, n_cache, rows):
    i = pl.program_id(0)
    length = meta_ref[0]
    qbase = meta_ref[1]

    @pl.when(i == 0)
    def _():
        m_sc[...] = jnp.full(m_sc.shape, NEG, jnp.float32)
        l_sc[...] = jnp.zeros(l_sc.shape, jnp.float32)
        acc_sc[...] = jnp.zeros(acc_sc.shape, jnp.float32)

    def step(kv_ref, allowed):
        parts = kv_ref.shape[0]
        for g in range(KVH):
            q = q_ref[g]
            k = jnp.concatenate([kv_ref[c, :, g * HD:(g + 1) * HD] for c in range(parts)], axis=0)
            v = jnp.concatenate(
                [kv_ref[c, :, KVH * HD + g * HD:KVH * HD + (g + 1) * HD] for c in range(parts)], axis=0
            )
            s = lax.dot_general(q, k, (((1,), (1,)), ((), ())), preferred_element_type=jnp.float32) * (HD ** -0.5)
            s = jnp.where(allowed, s, NEG)
            m_prev = m_sc[g]
            m_new = jnp.maximum(m_prev, jnp.max(s, axis=-1, keepdims=True))
            p = jnp.where(allowed, jnp.exp(s - m_new), 0.0)
            factor = jnp.exp(m_prev - m_new)
            l_sc[g] = l_sc[g] * factor + jnp.sum(p, axis=-1, keepdims=True)
            acc_sc[g] = acc_sc[g] * factor + jnp.dot(p.astype(jnp.bfloat16), v, preferred_element_type=jnp.float32)
            m_sc[g] = m_new

    @pl.when((i < n_cache) & (i * BLK < length))
    def _():
        key = i * BLK + lax.broadcasted_iota(jnp.int32, (rows, BLK), 1)
        step(cache_ref, key < length)

    j = i - n_cache
    tok = rows // (HEADS // KVH)

    @pl.when((i >= n_cache) & (j * BLK <= qbase + tok - 1))
    def _():
        key = j * BLK + lax.broadcasted_iota(jnp.int32, (rows, BLK), 1)
        qpos = qbase + lax.broadcasted_iota(jnp.int32, (rows, BLK), 0) % tok
        step(new_ref, key <= qpos)

    @pl.when(i == pl.num_programs(0) - 1)
    def _():
        for g in range(KVH):
            o_ref[g] = (acc_sc[g] / l_sc[g]).astype(o_ref.dtype)


def attention(queries, kv_all, length, qbase, chunk):
    shards, _, width = kv_all.shape
    rows = queries.shape[1]
    tok = kv_all.shape[1] - chunk
    cache_parts = BLK // chunk
    new_parts = BLK // tok
    n_cache = shards // cache_parts
    n_new = shards // new_parts
    meta = jnp.stack([length, qbase]).astype(jnp.int32)
    kern = functools.partial(attn_kernel, n_cache=n_cache, rows=rows)
    return pl.pallas_call(
        kern,
        out_shape=jax.ShapeDtypeStruct((KVH, rows, HD), jnp.bfloat16),
        grid_spec=pltpu.PrefetchScalarGridSpec(
            num_scalar_prefetch=1,
            grid=(n_cache + n_new,),
            in_specs=[
                pl.BlockSpec((KVH, rows, HD), lambda i, m: (0, 0, 0)),
                pl.BlockSpec(
                    (cache_parts, chunk, width), lambda i, m: (jnp.minimum(i, n_cache - 1), 0, 0)
                ),
                pl.BlockSpec(
                    (new_parts, tok, width), lambda i, m: (jnp.maximum(i - n_cache, 0), chunk // tok, 0)
                ),
            ],
            out_specs=pl.BlockSpec((KVH, rows, HD), lambda i, m: (0, 0, 0)),
            scratch_shapes=[
                pltpu.VMEM((KVH, rows, 1), jnp.float32),
                pltpu.VMEM((KVH, rows, 1), jnp.float32),
                pltpu.VMEM((KVH, rows, HD), jnp.float32),
            ],
        ),
        compiler_params=pltpu.CompilerParams(dimension_semantics=("arbitrary",)),
    )(meta, queries, kv_all, kv_all)

def ffn_kernel(x_ref, w_ref, o_ref):
    rows = x_ref.shape[0] * x_ref.shape[2]
    x = x_ref[...].reshape(rows, D)
    w = w_ref[0]
    dims = (((1,), (1,)), ((), ()))
    gate = lax.dot_general(x, w[:, :D], dims, preferred_element_type=jnp.float32)
    upper = lax.dot_general(x, w[:, D : 2 * D], dims, preferred_element_type=jnp.float32)
    inner = (gate / (1.0 + jnp.exp(-gate)) * upper).astype(jnp.bfloat16)
    out = jnp.dot(inner, w[:, 2 * D :], preferred_element_type=jnp.float32)
    o_ref[...] = out.astype(o_ref.dtype).reshape(o_ref.shape)


def experts(arrived, weights):
    groups, count, capacity, _ = arrived.shape
    hidden = weights.shape[1]
    return pl.pallas_call(
        ffn_kernel,
        out_shape=jax.ShapeDtypeStruct(arrived.shape, jnp.bfloat16),
        grid=(count,),
        in_specs=[
            pl.BlockSpec((groups, 1, capacity, D), lambda j: (0, j, 0, 0)),
            pl.BlockSpec((1, hidden, 3 * D), lambda j: (j, 0, 0)),
        ],
        out_specs=pl.BlockSpec((groups, 1, capacity, D), lambda j: (0, j, 0, 0)),
        compiler_params=pltpu.CompilerParams(
            dimension_semantics=("arbitrary",), vmem_limit_bytes=48 * 1024 * 1024
        ),
    )(arrived, weights)


def rms_scale(values, gain):
    floats = values.astype(jnp.float32)
    inverse = lax.rsqrt(jnp.mean(floats * floats, axis=-1, keepdims=True) + EPSILON)
    return (floats * inverse * gain).astype(jnp.bfloat16)


def rotate(values, positions):
    half_dim = values.shape[-1] // 2
    freqs = jnp.power(10000.0, -jnp.arange(half_dim, dtype=jnp.float32) / half_dim)
    angles = positions.astype(jnp.float32)[:, None] * freqs[None, :]
    cosine = jnp.cos(angles)[:, None, :]
    sine = jnp.sin(angles)[:, None, :]
    first = values[..., :half_dim]
    second = values[..., half_dim:]
    return jnp.concatenate(
        [first * cosine - second * sine, second * cosine + first * sine], axis=-1
    )


def local(
    hidden_states,
    attn_gain,
    w_qkv,
    w_out,
    kv_cache,
    cached_len,
    ffn_gain,
    w_router,
    expert_ids,
    w_gate,
    w_up,
    w_down,
):
    groups = HEADS // KVH
    tok_rows = hidden_states.shape[0]
    shard_pos = lax.axis_index("shard")
    length = cached_len[0]
    normed = rms_scale(hidden_states, attn_gain)
    qkv = jnp.dot(normed, w_qkv, preferred_element_type=jnp.float32)
    positions = length + shard_pos * tok_rows + jnp.arange(tok_rows, dtype=jnp.int32)
    queries = rotate(qkv[:, : HEADS * HD].reshape(tok_rows, HEADS, HD), positions).astype(
        jnp.bfloat16
    )
    new_keys = rotate(
        qkv[:, HEADS * HD : (HEADS + KVH) * HD].reshape(tok_rows, KVH, HD), positions
    ).astype(jnp.bfloat16)
    new_values = qkv[:, (HEADS + KVH) * HD :].astype(jnp.bfloat16)
    new_kv = jnp.concatenate([new_keys.reshape(tok_rows, KVH * HD), new_values], axis=1)
    joined = jnp.concatenate([kv_cache[0], new_kv], axis=0)
    kv_all = lax.all_gather(joined, "shard", axis=0, tiled=False)
    query_rows = queries.reshape(tok_rows, KVH, groups, HD).transpose(1, 2, 0, 3)
    query_rows = query_rows.reshape(KVH, groups * tok_rows, HD)
    attended = attention(query_rows, kv_all, length, shard_pos * tok_rows, kv_cache.shape[1])
    attended = attended.reshape(KVH, groups, tok_rows, HD).transpose(2, 0, 1, 3)
    attended = attended.reshape(tok_rows, HEADS * HD)
    mid = (
        hidden_states.astype(jnp.float32)
        + jnp.dot(attended, w_out, preferred_element_type=jnp.float32)
    ).astype(jnp.bfloat16)
    normed2 = rms_scale(mid, ffn_gain)
    group_count = lax.axis_size("req")
    local_experts = w_gate.shape[0]
    expert_count = local_experts * group_count
    capacity = min(tok_rows, 5 * tok_rows * TOP // (4 * expert_count))
    logits = jnp.dot(normed2, w_router, preferred_element_type=jnp.float32)
    picked = expert_ids[:, :, None] == jnp.arange(expert_count, dtype=jnp.int32)[None, None, :]
    chosen = jnp.sum(jnp.where(picked, logits[:, None, :], 0.0), axis=-1)
    gates = jax.nn.softmax(chosen, axis=-1)
    flat_hot = picked.reshape(tok_rows * TOP, expert_count).astype(jnp.int32)
    ranks = jnp.cumsum(flat_hot, axis=0) - flat_hot
    slot_rank = jnp.sum(ranks * flat_hot, axis=-1)
    slots = expert_ids.reshape(-1) * capacity + slot_rank
    slot_table = (
        slots.reshape(tok_rows, TOP)[:, :, None]
        == jnp.arange(expert_count * capacity, dtype=jnp.int32)[None, None, :]
    )
    placing = jnp.any(slot_table, axis=1).astype(jnp.bfloat16)
    outgoing = jnp.einsum("ts,td->sd", placing, normed2, preferred_element_type=jnp.float32).astype(
        jnp.bfloat16
    )
    outgoing = outgoing.reshape(group_count, local_experts, capacity, D)
    arrived = lax.all_to_all(outgoing, "req", split_axis=0, concat_axis=0, tiled=True)
    token_of = jnp.repeat(jnp.arange(tok_rows, dtype=jnp.float32), TOP)
    tags = jnp.zeros((expert_count * capacity, 2), jnp.float32)
    tags = tags.at[:, 0].set(-1.0).at[slots].set(jnp.stack([token_of, gates.reshape(-1)], axis=-1))
    tags = tags.reshape(group_count, local_experts * capacity, 2)
    tags = lax.all_to_all(tags, "req", split_axis=0, concat_axis=0, tiled=True)
    weights = jnp.concatenate([w_gate, w_up, w_down], axis=-1)
    weights = lax.all_gather(weights, "shard", axis=1, tiled=True)
    expert_rows = experts(arrived, weights).astype(jnp.float32)
    expert_rows = expert_rows.reshape(group_count, local_experts * capacity, D)
    owner = tags[..., 0].astype(jnp.int32)
    weighting = jnp.where(
        owner[:, None, :] == jnp.arange(tok_rows, dtype=jnp.int32)[None, :, None], tags[:, None, :, 1], 0.0
    )
    partial = jnp.einsum(
        "stm,smd->std", weighting, expert_rows, preferred_element_type=jnp.float32,
        precision=lax.Precision.HIGHEST,
    )
    returned = lax.all_to_all(partial.astype(jnp.bfloat16), "req", split_axis=0, concat_axis=0, tiled=True)
    mixture = jnp.sum(returned.astype(jnp.float32), axis=0)
    return (mid.astype(jnp.float32) + mixture).astype(jnp.bfloat16)


def solution(mesh):
    return jax.shard_map(
        local,
        mesh=mesh,
        in_specs=(
            P(("req", "shard"), None),
            P(),
            P(),
            P(),
            P("req", "shard", None),
            P("req"),
            P(),
            P(),
            P(("req", "shard"), None),
            P("req", "shard", None),
            P("req", "shard", None),
            P("req", "shard", None),
        ),
        out_specs=P(("req", "shard"), None),
        check_vma=False,
    )
```

profile of v0, /device:TPU:30, one launch (start us, length us, event | category | flops | bytes accessed | tf_op | source)
XLA Modules:
  0.0 322.5 jit_solution(3203083420044820654)
XLA Ops:
  6.6 1.2 fusion.3
  7.8 4.7 %fusion.7 = f32[128,2560]{1,0:T(8,128)S(1)} fusion(bf16[1536,2560]{1,0:T(8,128)(2,1)} %param.16, bf16[128,1536]{1,0:T(8,128)(2,1)} %param.14, f32[1536]{0:T(1024)} %param.15, f32[128]{0:T(128)S(1)} %add_rsqrt_fusion.1), kind=kOutput, calls=%fused_computation.22 | convolution fusion | flops 1007419392 | bytes 9574912 | tf_op jit(solution)/shard_map/dot_general | solution.py:176
  13.3 0.1 copy.67
  13.4 0.1 multiply_cosine_fusion
  13.7 1.0 maximum_maximum_fusion
  14.8 2.4 pad_maximum_fusion
  17.6 0.3 copy.64
  18.0 0.4 copy.65
  18.4 0.4 copy.66
  18.9 11.3 %reduce-window.6 = s32[40,8,128]{2,1,0:T(8,128)S(1)} reduce-window(s32[40,8,128]{2,1,0:T(8,128)S(1)} %fusion.17, s32[]{:T(128)} %constant.62.clone.1), window={size=1x1x128 pad=0_0x0_0x127_0}, to_apply=%region_1.0 | reduce-window | flops 5201920 | bytes 327684 | tf_op jit(solution)/shard_map/reduce-window
  30.3 0.1 copy.73
  30.9 0.7 pad_add_fusion.meta_ref
  31.6 1.4 pad_maximum_fusion.1
  33.0 1.6 fusion
  34.6 70.1 %all-gather.6.cloned.1.call-done = bf16[6144,1024]{1,0:T(8,128)(2,1)} async-done(((bf16[384,1024]{1,0:T(8,128)(2,1)}), bf16[6144,1024]{1,0:T(8,128)(2,1)}) %all-gather.6.cloned.1.call-update) | async-done | bytes 12582928 | tf_op jit(solution)/shard_map/all_gather | solution.py:187
  104.7 41.3 %shard_map.118 = bf16[8,384,64]{2,1,0:T(8,128)(2,1)} custom-call(s32[2]{0:T(128)} %pad_add_fusion.meta_ref, bf16[8,384,64]{2,1,0:T(8,128)(2,1)} %bitcast.56, bf16[16,384,1024]{2,1,0:T(8,128)(2,1)} %bitcast.51, bf16[16,384,1024]{2,1,0:T(8,128)(2,1)} %bitcast.52), custom_call_target="tpu_custom_call" | custom-call | tf_op jit(solution)/shard_map/pallas_call | solution.py:83
  146.0 1.4 copy.69
  147.4 3.3 %multiply_reduce_fusion = (f32[128]{0:T(128)S(1)}, f32[128,1536]{1,0:T(8,128)S(1)}) fusion(bf16[128,1536]{0,1:T(8,128)(2,1)S(1)} %bitcast.58, bf16[1536,1536]{1,0:T(8,128)(2,1)} %param.17, bf16[128,1536]{1,0:T(8,128)(2,1)S(1)} %copy-done.3), kind=kOutput, calls=%fused_computation.19 | convolution fusion | flops 605159296 | bytes 6291968 | tf_op jit(solution)/shard_map/dot_general | solution.py:195
  150.8 0.3 fusion.23
  151.4 0.2 copy.76
  151.6 3.4 %scatter_fusion = f32[1280,2]{1,0:T(8,128)S(1)} fusion(f32[1280,2]{1,0:T(8,128)S(1)} %copy-done.2, s32[1024]{0:T(1024)S(1)} %bitcast.66, f32[1024,2]{1,0:T(8,128)S(1)} %copy.76), kind=kCustom, calls=%fused_computation | custom fusion | bytes 28672 | tf_op jit(solution)/shard_map/scatter | solution.py:222
  155.0 0.9 copy.77
  155.9 44.6 %all-to-all-start = ((f32[8,160,2]{1,2,0:T(2,128)}), f32[8,160,2]{1,2,0:T(2,128)S(1)}, u32[]{:S(2)}, u32[]{:S(2)}) async-start(f32[8,160,2]{1,2,0:T(2,128)} %copy.77), calls=%async_computation | async-start | bytes 32768 | tf_op jit(solution)/shard_map/all_to_all | solution.py:224
  200.6 3.3 %convolution_convert_fusion = bf16[1280,1536]{1,0:T(8,128)(2,1)} fusion(pred[128,1280]{1,0:T(8,128)(4,1)S(1)} %fusion, f32[128,1536]{1,0:T(8,128)S(1)} %get-tuple-element.28, f32[1536]{0:T(1024)S(1)} %copy-done.6, f32[128]{0:T(128)S(1)} %add_rsqrt_fusion), kind=kOutput, calls=%fused_computation.1 | convolution fusion | flops 505872384 | bytes 4889088 | tf_op jit(solution)/shard_map/ts,td->sd/dot_general | solution.py:215
  203.8 2.1 all-to-all-done
  205.9 4.6 %all-to-all-start.1 = ((bf16[8,5,32,1536]{3,2,1,0:T(8,128)(2,1)}), bf16[8,5,32,1536]{3,2,1,0:T(8,128)(2,1)}, u32[]{:S(2)}, u32[]{:S(2)}) async-start(bf16[8,5,32,1536]{3,2,1,0:T(8,128)(2,1)} %bitcast.54), calls=%async_computation.1 | async-start | bytes 7864320 | tf_op jit(solution)/shard_map/all_to_all | solution.py:219
  210.6 46.8 %all-to-all-done.1.x_ref = bf16[8,5,32,1536]{3,2,1,0:T(8,128)(2,1)} async-done(((bf16[8,5,32,1536]{3,2,1,0:T(8,128)(2,1)}), bf16[8,5,32,1536]{3,2,1,0:T(8,128)(2,1)}, u32[]{:S(2)}, u32[]{:S(2)}) %all-to-all-start.1) | async-done | bytes 3932192 | tf_op jit(solution)/shard_map/all_to_all | solution.py:219
  257.4 12.5 %shard_map.119 = bf16[8,5,32,1536]{3,2,1,0:T(8,128)(2,1)S(1)} custom-call(bf16[8,5,32,1536]{3,2,1,0:T(8,128)(2,1)} %all-to-all-done.1.x_ref, bf16[5,512,4608]{2,1,0:T(8,128)(2,1)} %all-gather.4.cloned.1.call-done.w_ref), custom_call_target="tpu_custom_call" | custom-call | tf_op jit(solution)/shard_map/pallas_call | solution.py:123
  269.9 3.5 %convolution_convert_fusion.1 = bf16[8,128,1536]{2,1,0:T(8,128)(2,1)S(1)} fusion(bf16[8,160,1536]{2,1,0:T(8,128)(2,1)S(1)} %bitcast.50, f32[8,160]{1,0:T(8,128)S(1)} %get-tuple-element.29, s32[8,160]{1,0:T(8,128)S(1)} %get-tuple-element.30), kind=kOutput, calls=%fused_computation.5 | convolution fusion | flops 3021799424 | bytes 7088128 | tf_op jit(solution)/shard_map/stm,smd->std/dot_general | solution.py:233
  273.3 41.0 %all_to_all.15 = bf16[8,128,1536]{2,1,0:T(8,128)(2,1)S(1)} all-to-all(bf16[8,128,1536]{2,1,0:T(8,128)(2,1)S(1)} %convolution_convert_fusion.1), channel_id=1, replica_groups=mesh['req'=8,'shard'=16] {'req'}, dimensions={0} | all-to-all | bytes 6291456 | tf_op jit(solution)/shard_map/all_to_all | solution.py:237
  314.4 0.4 convert_reduce_fusion
  314.8 0.9 add_convert_fusion
  (57 shorter events, 1.8 us)
Async XLA Ops:
  6.5 144.2 %copy-start = (bf16[1536,40]{0,1:T(8,128)(2,1)S(1)}, bf16[1536,40]{0,1:T(8,128)(2,1)}, u32[]{:S(2)}) copy-start(bf16[1536,40]{0,1:T(8,128)(2,1)} %param.21) | copy-start | bytes 368644
  6.5 98.1 %all-gather.6.cloned.1.call-start = ((), (), s32[]{:S(2)}) async-start(), calls=%async_computation.4 | async-start | bytes 13369344 | tf_op jit(solution)/shard_map/all_gather | solution.py:187
  7.8 6.0 %copy-start.4 = (bf16[1,256,1024]{2,1,0:T(8,128)(2,1)S(1)}, bf16[1,256,1024]{2,1,0:T(8,128)(2,1)}, u32[]{:S(2)}) copy-start(bf16[1,256,1024]{2,1,0:T(8,128)(2,1)} %param.18) | copy-start | bytes 1572868
  12.5 2.3 copy-start.5
  14.7 2.6 copy-start.7
  14.8 242.6 %all-gather.4.cloned.1.call-start = ((), (), s32[]{:S(2)}) async-start(), calls=%async_computation.3 | async-start | bytes 25067520 | tf_op jit(solution)/shard_map/all_gather | solution.py:226
  104.7 42.7 %copy-start.3 = (bf16[128,1536]{1,0:T(8,128)(2,1)S(1)}, bf16[128,1536]{1,0:T(8,128)(2,1)}, u32[]{:S(2)}) copy-start(bf16[128,1536]{1,0:T(8,128)(2,1)} %param.14) | copy-start | bytes 1179652
  147.4 3.3 %copy-start.6 = (f32[1536]{0:T(1024)S(1)}, f32[1536]{0:T(1024)}, u32[]{:S(2)}) copy-start(f32[1536]{0:T(1024)} %param.20) | copy-start | bytes 18436
  147.4 4.2 %copy-start.2 = (f32[1280,2]{1,0:T(8,128)S(1)}, f32[1280,2]{1,0:T(8,128)}, u32[]{:S(2)}) copy-start(f32[1280,2]{1,0:T(8,128)} %constant.60.clone.1) | copy-start | bytes 30724
  155.9 50.0 %all-to-all-start = ((f32[8,160,2]{1,2,0:T(2,128)}), f32[8,160,2]{1,2,0:T(2,128)S(1)}, u32[]{:S(2)}, u32[]{:S(2)}) async-start(f32[8,160,2]{1,2,0:T(2,128)} %copy.77), calls=%async_computation | async-start | bytes 32768 | tf_op jit(solution)/shard_map/all_to_all | solution.py:224
  205.9 51.4 %all-to-all-start.1 = ((bf16[8,5,32,1536]{3,2,1,0:T(8,128)(2,1)}), bf16[8,5,32,1536]{3,2,1,0:T(8,128)(2,1)}, u32[]{:S(2)}, u32[]{:S(2)}) async-start(bf16[8,5,32,1536]{3,2,1,0:T(8,128)(2,1)} %bitcast.54), calls=%async_computation.1 | async-start | bytes 7864320 | tf_op jit(solution)/shard_map/all_to_all | solution.py:219
  273.3 42.3 %copy-start.1 = (bf16[1536,40]{0,1:T(8,128)(2,1)S(1)}, bf16[1536,40]{0,1:T(8,128)(2,1)}, u32[]{:S(2)}) copy-start(bf16[1536,40]{0,1:T(8,128)(2,1)} %param.21) | copy-start | bytes 368644
Sparse Core Ops, SparseCore 0:
  14.9 89.7 all-gather.5
  106.8 145.6 all-gather.3
where the time goes:
time: 325 us; the launch traced here: 323 us
  waiting for transfers between devices  119 us (37%)
  Pallas kernels  53.8 us (17%)
  starting transfers between devices  49.2 us (15%)
  blocking collectives  41 us (13%)
  other arithmetic  21.5 us (7%)
  matrix products  15 us (5%)
  between operations  14.5 us (4%)
  local copies, waits for them, and re-layouts  8.45 us (3%)
    all_gather x1, waiting for transfers between devices, local(): kv_all = lax.all_gather(joined, 'shard', axis=0, tiled=False)  70.1 us
    all_to_all x1, waiting for transfers between devices, local(): lax.all_to_all(outgoing, 'req', split_axis=0, concat_axis=0, tiled=True)  46.8 us
    all_to_all x1, starting transfers between devices, local(): tags = lax.all_to_all(tags, 'req', split_axis=0, concat_axis=0, tiled=True)  44.6 us
    pallas_call x1, Pallas kernels, attention(): pl.pallas_call(kern, out_shape=jax.ShapeDtypeStruct((KVH, rows, HD), jnp....  41.3 us
    all_to_all x1, blocking collectives, local(): lax.all_to_all(partial.astype(jnp.bfloat16), 'req', split_axis=0, concat_...  41 us
    pallas_call x1, Pallas kernels, experts(): pl.pallas_call(ffn_kernel, out_shape=jax.ShapeDtypeStruct(arrived.shape,...  12.5 us
    another operation x5, other arithmetic  11.6 us
  transfers between devices with their start and end apart: 4, of which 3 were waited for; matrix products, arithmetic and copies ran while one was open for 10% of the time, Pallas kernels for 13%

commit v1 on v0

--- a/solution.py
+++ b/solution.py
@@ -105,35 +105,55 @@
         compiler_params=pltpu.CompilerParams(dimension_semantics=("arbitrary",)),
     )(meta, queries, kv_all, kv_all)
 
-def ffn_kernel(x_ref, w_ref, o_ref):
-    rows = x_ref.shape[0] * x_ref.shape[2]
+def ffn_kernel(x_ref, w_ref, g_ref, o_ref, acc_ref):
+    j = pl.program_id(0)
+    groups, _, capacity, _ = x_ref.shape
+    rows = groups * capacity
     x = x_ref[...].reshape(rows, D)
     w = w_ref[0]
     dims = (((1,), (1,)), ((), ()))
     gate = lax.dot_general(x, w[:, :D], dims, preferred_element_type=jnp.float32)
     upper = lax.dot_general(x, w[:, D : 2 * D], dims, preferred_element_type=jnp.float32)
     inner = (gate / (1.0 + jnp.exp(-gate)) * upper).astype(jnp.bfloat16)
-    out = jnp.dot(inner, w[:, 2 * D :], preferred_element_type=jnp.float32)
-    o_ref[...] = out.astype(o_ref.dtype).reshape(o_ref.shape)
-
-
-def experts(arrived, weights):
+    out = jnp.dot(inner, w[:, 2 * D :], preferred_element_type=jnp.float32).astype(jnp.bfloat16)
+
+    @pl.when(j == 0)
+    def _():
+        acc_ref[...] = jnp.zeros(acc_ref.shape, jnp.float32)
+
+    for s in range(groups):
+        share = g_ref[0, s]
+        high = share.astype(jnp.bfloat16)
+        low = (share - high.astype(jnp.float32)).astype(jnp.bfloat16)
+        rows_s = out[s * capacity : (s + 1) * capacity]
+        acc_ref[s] += jnp.dot(high, rows_s, preferred_element_type=jnp.float32) + jnp.dot(
+            low, rows_s, preferred_element_type=jnp.float32
+        )
+
+    @pl.when(j == pl.num_programs(0) - 1)
+    def _():
+        o_ref[...] = acc_ref[...].astype(o_ref.dtype)
+
+
+def experts(arrived, weights, shares):
     groups, count, capacity, _ = arrived.shape
     hidden = weights.shape[1]
+    tokens = shares.shape[2]
     return pl.pallas_call(
         ffn_kernel,
-        out_shape=jax.ShapeDtypeStruct(arrived.shape, jnp.bfloat16),
+        out_shape=jax.ShapeDtypeStruct((groups, tokens, D), jnp.bfloat16),
         grid=(count,),
         in_specs=[
             pl.BlockSpec((groups, 1, capacity, D), lambda j: (0, j, 0, 0)),
             pl.BlockSpec((1, hidden, 3 * D), lambda j: (j, 0, 0)),
+            pl.BlockSpec((1, groups, tokens, capacity), lambda j: (j, 0, 0, 0)),
         ],
-        out_specs=pl.BlockSpec((groups, 1, capacity, D), lambda j: (0, j, 0, 0)),
+        out_specs=pl.BlockSpec((groups, tokens, D), lambda j: (0, 0, 0)),
+        scratch_shapes=[pltpu.VMEM((groups, tokens, D), jnp.float32)],
         compiler_params=pltpu.CompilerParams(
             dimension_semantics=("arbitrary",), vmem_limit_bytes=48 * 1024 * 1024
         ),
-    )(arrived, weights)
-
+    )(arrived, weights, shares)
 
 def rms_scale(values, gain):
     floats = values.astype(jnp.float32)
@@ -224,17 +244,13 @@
     tags = lax.all_to_all(tags, "req", split_axis=0, concat_axis=0, tiled=True)
     weights = jnp.concatenate([w_gate, w_up, w_down], axis=-1)
     weights = lax.all_gather(weights, "shard", axis=1, tiled=True)
-    expert_rows = experts(arrived, weights).astype(jnp.float32)
-    expert_rows = expert_rows.reshape(group_count, local_experts * capacity, D)
     owner = tags[..., 0].astype(jnp.int32)
     weighting = jnp.where(
         owner[:, None, :] == jnp.arange(tok_rows, dtype=jnp.int32)[None, :, None], tags[:, None, :, 1], 0.0
     )
-    partial = jnp.einsum(
-        "stm,smd->std", weighting, expert_rows, preferred_element_type=jnp.float32,
-        precision=lax.Precision.HIGHEST,
-    )
-    returned = lax.all_to_all(partial.astype(jnp.bfloat16), "req", split_axis=0, concat_axis=0, tiled=True)
+    shares = weighting.reshape(group_count, tok_rows, local_experts, capacity).transpose(2, 0, 1, 3)
+    partial = experts(arrived, weights, shares)
+    returned = lax.all_to_all(partial, "req", split_axis=0, concat_axis=0, tiled=True)
     mixture = jnp.sum(returned.astype(jnp.float32), axis=0)
     return (mid.astype(jnp.float32) + mixture).astype(jnp.bfloat16)
 

time: 325 us -> 329 us (1.012)
  Pallas kernels: 53.8 us -> 95.1 us
  starting transfers between devices: 49.2 us -> 14.4 us
    all_to_all x1, starting transfers between devices: 44.6 us -> 9.83 us  [local(): tags = lax.all_to_all(tags, 'req', split_axis=0, concat_axis=0, tiled=True)]
    pallas_call x1, Pallas kernels: 41.3 us -> 75.4 us  [attention(): pl.pallas_call(kern, out_shape=jax.ShapeDtypeStruct((KVH, rows, HD), jnp....]
    pallas_call x1, Pallas kernels: 12.5 us -> 19.7 us  [experts(): pl.pallas_call(ffn_kernel, out_shape=jax.ShapeDtypeStruct((groups, tokens...]
    dot_general x1 -> x0, matrix products: 3.45 us -> none  [local(): jnp.einsum('stm,smd->std', weighting, expert_rows, preferred_element_type...]
  transfers between devices with their start and end apart: 4 -> 4, of which waited for: 3 -> 3; matrix products, arithmetic and copies ran while one was open for 10% -> 10% of each run, Pallas kernels for 13% -> 23%
where the time goes in v1:
time: 329 us; the launch traced here: 326 us
  waiting for transfers between devices  118 us (36%)
  Pallas kernels  95.1 us (29%)
  blocking collectives  41 us (12%)
  other arithmetic  21.9 us (7%)
  between operations  14.5 us (4%)
  starting transfers between devices  14.4 us (4%)
  matrix products  11.8 us (4%)
  local copies, waits for them, and re-layouts  8.63 us (3%)
    pallas_call x1, Pallas kernels, attention(): pl.pallas_call(kern, out_shape=jax.ShapeDtypeStruct((KVH, rows, HD), jnp....  75.4 us
    all_gather x1, waiting for transfers between devices, local(): kv_all = lax.all_gather(joined, 'shard', axis=0, tiled=False)  70.1 us
    all_to_all x1, waiting for transfers between devices, local(): lax.all_to_all(outgoing, 'req', split_axis=0, concat_axis=0, tiled=True)  46.2 us
    all_to_all x1, blocking collectives, local(): lax.all_to_all(partial, 'req', split_axis=0, concat_axis=0, tiled=True)  41 us
    pallas_call x1, Pallas kernels, experts(): pl.pallas_call(ffn_kernel, out_shape=jax.ShapeDtypeStruct((groups, tokens...  19.7 us
    another operation x5, other arithmetic  11.6 us
    all_to_all x1, starting transfers between devices, local(): tags = lax.all_to_all(tags, 'req', split_axis=0, concat_axis=0, tiled=True)  9.83 us
  transfers between devices with their start and end apart: 4, of which 3 were waited for; matrix products, arithmetic and copies ran while one was open for 10% of the time, Pallas kernels for 23%

profile of v1, /device:TPU:30, one launch (start us, length us, event | category | flops | bytes accessed | tf_op | source)
XLA Modules:
  0.0 325.8 jit_solution(423304327878414429)
XLA Ops:
  6.6 1.2 fusion.4
  7.8 4.7 %fusion.7 = f32[128,2560]{1,0:T(8,128)S(1)} fusion(bf16[1536,2560]{1,0:T(8,128)(2,1)} %param.16, bf16[128,1536]{1,0:T(8,128)(2,1)} %param.14, f32[1536]{0:T(1024)} %param.15, f32[128]{0:T(128)S(1)} %add_rsqrt_fusion.1), kind=kOutput, calls=%fused_computation.21 | convolution fusion | flops 1007419392 | bytes 9574912 | tf_op jit(solution)/shard_map/dot_general | solution.py:196
  13.3 0.1 copy.70
  13.4 0.1 multiply_cosine_fusion
  13.7 1.0 maximum_maximum_fusion
  14.8 2.4 pad_maximum_fusion
  17.6 0.3 copy.67
  18.0 0.4 copy.68
  18.4 0.4 copy.69
  18.9 11.3 %reduce-window.6 = s32[40,8,128]{2,1,0:T(8,128)S(1)} reduce-window(s32[40,8,128]{2,1,0:T(8,128)S(1)} %fusion.14, s32[]{:T(128)} %constant.61.clone.1), window={size=1x1x128 pad=0_0x0_0x127_0}, to_apply=%region_1.0 | reduce-window | flops 5201920 | bytes 327684 | tf_op jit(solution)/shard_map/reduce-window
  30.3 0.1 copy.76
  30.9 0.7 pad_add_fusion.meta_ref
  31.6 1.4 pad_maximum_fusion.1
  33.0 1.6 fusion
  34.6 70.1 %all-gather.6.cloned.1.call-done = bf16[6144,1024]{1,0:T(8,128)(2,1)} async-done(((bf16[384,1024]{1,0:T(8,128)(2,1)}), bf16[6144,1024]{1,0:T(8,128)(2,1)}) %all-gather.6.cloned.1.call-update) | async-done | bytes 12582928 | tf_op jit(solution)/shard_map/all_gather | solution.py:207
  104.7 75.4 %shard_map.118 = bf16[8,384,64]{2,1,0:T(8,128)(2,1)} custom-call(s32[2]{0:T(128)} %pad_add_fusion.meta_ref, bf16[8,384,64]{2,1,0:T(8,128)(2,1)} %bitcast.51, bf16[16,384,1024]{2,1,0:T(8,128)(2,1)} %bitcast.46, bf16[16,384,1024]{2,1,0:T(8,128)(2,1)} %bitcast.47), custom_call_target="tpu_custom_call" | custom-call | tf_op jit(solution)/shard_map/pallas_call | solution.py:83
  180.1 1.4 copy.72
  181.5 3.5 %multiply_reduce_fusion = (f32[128]{0:T(128)S(1)}, f32[128,1536]{1,0:T(8,128)S(1)}) fusion(bf16[128,1536]{0,1:T(8,128)(2,1)S(1)} %bitcast.53, bf16[1536,1536]{1,0:T(8,128)(2,1)} %param.17, bf16[128,1536]{1,0:T(8,128)(2,1)S(1)} %copy-done.3), kind=kOutput, calls=%fused_computation.20 | convolution fusion | flops 605159296 | bytes 6291968 | tf_op jit(solution)/shard_map/dot_general | solution.py:215
  185.1 0.3 fusion.19
  185.7 0.2 copy.79
  185.9 3.4 %scatter_fusion = f32[1280,2]{1,0:T(8,128)S(1)} fusion(f32[1280,2]{1,0:T(8,128)S(1)} %copy-done.2, s32[1024]{0:T(1024)S(1)} %bitcast.63, f32[1024,2]{1,0:T(8,128)S(1)} %copy.79), kind=kCustom, calls=%fused_computation | custom fusion | bytes 28672 | tf_op jit(solution)/shard_map/scatter | solution.py:242
  189.3 0.9 copy.80
  190.2 9.8 %all-to-all-start.1 = ((f32[8,160,2]{1,2,0:T(2,128)}), f32[8,160,2]{1,2,0:T(2,128)S(1)}, u32[]{:S(2)}, u32[]{:S(2)}) async-start(f32[8,160,2]{1,2,0:T(2,128)} %copy.80), calls=%async_computation.1 | async-start | bytes 32768 | tf_op jit(solution)/shard_map/all_to_all | solution.py:244
  200.1 3.3 %convolution_convert_fusion = bf16[1280,1536]{1,0:T(8,128)(2,1)} fusion(pred[128,1280]{1,0:T(8,128)(4,1)S(1)} %fusion, f32[128,1536]{1,0:T(8,128)S(1)} %get-tuple-element.26, f32[1536]{0:T(1024)S(1)} %copy-done.6, f32[128]{0:T(128)S(1)} %add_rsqrt_fusion), kind=kOutput, calls=%fused_computation.1 | convolution fusion | flops 505872384 | bytes 4889088 | tf_op jit(solution)/shard_map/ts,td->sd/dot_general | solution.py:235
  203.3 2.1 all-to-all-done.1
  205.4 4.6 %all-to-all-start = ((bf16[8,5,32,1536]{3,2,1,0:T(8,128)(2,1)}), bf16[8,5,32,1536]{3,2,1,0:T(8,128)(2,1)}, u32[]{:S(2)}, u32[]{:S(2)}) async-start(bf16[8,5,32,1536]{3,2,1,0:T(8,128)(2,1)} %bitcast.49), calls=%async_computation | async-start | bytes 7864320 | tf_op jit(solution)/shard_map/all_to_all | solution.py:239
  210.2 0.4 fusion.1.g_ref
  210.6 46.2 %all-to-all-done.x_ref = bf16[8,5,32,1536]{3,2,1,0:T(8,128)(2,1)} async-done(((bf16[8,5,32,1536]{3,2,1,0:T(8,128)(2,1)}), bf16[8,5,32,1536]{3,2,1,0:T(8,128)(2,1)}, u32[]{:S(2)}, u32[]{:S(2)}) %all-to-all-start) | async-done | bytes 3932192 | tf_op jit(solution)/shard_map/all_to_all | solution.py:239
  256.8 19.7 %shard_map.119 = bf16[8,128,1536]{2,1,0:T(8,128)(2,1)S(1)} custom-call(bf16[8,5,32,1536]{3,2,1,0:T(8,128)(2,1)} %all-to-all-done.x_ref, bf16[5,512,4608]{2,1,0:T(8,128)(2,1)} %all-gather.4.cloned.1.call-done.w_ref, f32[5,8,128,32]{3,2,1,0:T(8,128)S(1)} %fusion.1.g_ref), custom_call_target="tpu_custom_call" | custom-call | tf_op jit(solution)/shard_map/pallas_call | solution.py:142
  276.6 41.0 %all_to_all.15 = bf16[8,128,1536]{2,1,0:T(8,128)(2,1)S(1)} all-to-all(bf16[8,128,1536]{2,1,0:T(8,128)(2,1)S(1)} %shard_map.119), channel_id=1, replica_groups=mesh['req'=8,'shard'=16] {'req'}, dimensions={0} | all-to-all | bytes 6291456 | tf_op jit(solution)/shard_map/all_to_all | solution.py:253
  317.6 0.4 convert_reduce_fusion
  318.1 0.9 add_convert_fusion
  (61 shorter events, 2.0 us)
Async XLA Ops:
  6.5 178.5 %copy-start = (bf16[1536,40]{0,1:T(8,128)(2,1)S(1)}, bf16[1536,40]{0,1:T(8,128)(2,1)}, u32[]{:S(2)}) copy-start(bf16[1536,40]{0,1:T(8,128)(2,1)} %param.21) | copy-start | bytes 368644
  6.5 98.1 %all-gather.6.cloned.1.call-start = ((), (), s32[]{:S(2)}) async-start(), calls=%async_computation.4 | async-start | bytes 13369344 | tf_op jit(solution)/shard_map/all_gather | solution.py:207
  7.8 6.0 %copy-start.4 = (bf16[1,256,1024]{2,1,0:T(8,128)(2,1)S(1)}, bf16[1,256,1024]{2,1,0:T(8,128)(2,1)}, u32[]{:S(2)}) copy-start(bf16[1,256,1024]{2,1,0:T(8,128)(2,1)} %param.18) | copy-start | bytes 1572868
  12.5 2.3 copy-start.5
  14.7 2.6 copy-start.7
  14.8 242.1 %all-gather.4.cloned.1.call-start = ((), (), s32[]{:S(2)}) async-start(), calls=%async_computation.3 | async-start | bytes 25067520 | tf_op jit(solution)/shard_map/all_gather | solution.py:246
  104.7 76.8 %copy-start.3 = (bf16[128,1536]{1,0:T(8,128)(2,1)S(1)}, bf16[128,1536]{1,0:T(8,128)(2,1)}, u32[]{:S(2)}) copy-start(bf16[128,1536]{1,0:T(8,128)(2,1)} %param.14) | copy-start | bytes 1179652
  181.5 3.5 %copy-start.6 = (f32[1536]{0:T(1024)S(1)}, f32[1536]{0:T(1024)}, u32[]{:S(2)}) copy-start(f32[1536]{0:T(1024)} %param.20) | copy-start | bytes 18436
  181.5 4.4 %copy-start.2 = (f32[1280,2]{1,0:T(8,128)S(1)}, f32[1280,2]{1,0:T(8,128)}, u32[]{:S(2)}) copy-start(f32[1280,2]{1,0:T(8,128)} %constant.63.clone.1) | copy-start | bytes 30724
  190.2 15.2 %all-to-all-start.1 = ((f32[8,160,2]{1,2,0:T(2,128)}), f32[8,160,2]{1,2,0:T(2,128)S(1)}, u32[]{:S(2)}, u32[]{:S(2)}) async-start(f32[8,160,2]{1,2,0:T(2,128)} %copy.80), calls=%async_computation.1 | async-start | bytes 32768 | tf_op jit(solution)/shard_map/all_to_all | solution.py:244
  205.4 51.4 %all-to-all-start = ((bf16[8,5,32,1536]{3,2,1,0:T(8,128)(2,1)}), bf16[8,5,32,1536]{3,2,1,0:T(8,128)(2,1)}, u32[]{:S(2)}, u32[]{:S(2)}) async-start(bf16[8,5,32,1536]{3,2,1,0:T(8,128)(2,1)} %bitcast.49), calls=%async_computation | async-start | bytes 7864320 | tf_op jit(solution)/shard_map/all_to_all | solution.py:239
  276.6 42.3 %copy-start.1 = (bf16[1536,40]{0,1:T(8,128)(2,1)S(1)}, bf16[1536,40]{0,1:T(8,128)(2,1)}, u32[]{:S(2)}) copy-start(bf16[1536,40]{0,1:T(8,128)(2,1)} %param.21) | copy-start | bytes 368644
Sparse Core Ops, SparseCore 0:
  14.9 89.7 all-gather.5
  106.8 145.6 all-gather.3

commit v2 on v0

--- a/solution.py
+++ b/solution.py
@@ -232,7 +232,7 @@
     )
     partial = jnp.einsum(
         "stm,smd->std", weighting, expert_rows, preferred_element_type=jnp.float32,
-        precision=lax.Precision.HIGHEST,
+        precision=lax.Precision.HIGH,
     )
     returned = lax.all_to_all(partial.astype(jnp.bfloat16), "req", split_axis=0, concat_axis=0, tiled=True)
     mixture = jnp.sum(returned.astype(jnp.float32), axis=0)

time: 325 us -> 324 us (level)
  starting transfers between devices: 49.2 us -> 14.9 us
  Pallas kernels: 53.8 us -> 87.9 us
    all_to_all x1, starting transfers between devices: 44.6 us -> 10.3 us  [local(): tags = lax.all_to_all(tags, 'req', split_axis=0, concat_axis=0, tiled=True)]
    pallas_call x1, Pallas kernels: 41.3 us -> 75.4 us  [attention(): pl.pallas_call(kern, out_shape=jax.ShapeDtypeStruct((KVH, rows, HD), jnp....]
  transfers between devices with their start and end apart: 4 -> 4, of which waited for: 3 -> 3; matrix products, arithmetic and copies ran while one was open for 10% -> 10% of each run, Pallas kernels for 13% -> 23%
where the time goes in v2:
time: 324 us; the launch traced here: 322 us
  waiting for transfers between devices  119 us (37%)
  Pallas kernels  87.9 us (27%)
  blocking collectives  41 us (13%)
  other arithmetic  21.5 us (7%)
  starting transfers between devices  14.9 us (5%)
  between operations  14.5 us (4%)
  matrix products  14.4 us (4%)
  local copies, waits for them, and re-layouts  8.45 us (3%)
    pallas_call x1, Pallas kernels, attention(): pl.pallas_call(kern, out_shape=jax.ShapeDtypeStruct((KVH, rows, HD), jnp....  75.4 us
    all_gather x1, waiting for transfers between devices, local(): kv_all = lax.all_gather(joined, 'shard', axis=0, tiled=False)  70.1 us
    all_to_all x1, waiting for transfers between devices, local(): lax.all_to_all(outgoing, 'req', split_axis=0, concat_axis=0, tiled=True)  46.8 us
    all_to_all x1, blocking collectives, local(): lax.all_to_all(partial.astype(jnp.bfloat16), 'req', split_axis=0, concat_...  41 us
    pallas_call x1, Pallas kernels, experts(): pl.pallas_call(ffn_kernel, out_shape=jax.ShapeDtypeStruct(arrived.shape,...  12.5 us
    another operation x5, other arithmetic  11.6 us
    all_to_all x1, starting transfers between devices, local(): tags = lax.all_to_all(tags, 'req', split_axis=0, concat_axis=0, tiled=True)  10.3 us
  transfers between devices with their start and end apart: 4, of which 3 were waited for; matrix products, arithmetic and copies ran while one was open for 10% of the time, Pallas kernels for 23%

profile of v2, /device:TPU:30, one launch (start us, length us, event | category | flops | bytes accessed | tf_op | source)
XLA Modules:
  0.0 321.7 jit_solution(6428556143977097804)
XLA Ops:
  6.6 1.2 fusion.3
  7.8 4.7 %fusion.7 = f32[128,2560]{1,0:T(8,128)S(1)} fusion(bf16[1536,2560]{1,0:T(8,128)(2,1)} %param.16, bf16[128,1536]{1,0:T(8,128)(2,1)} %param.14, f32[1536]{0:T(1024)} %param.15, f32[128]{0:T(128)S(1)} %add_rsqrt_fusion.1), kind=kOutput, calls=%fused_computation.22 | convolution fusion | flops 1007419392 | bytes 9574912 | tf_op jit(solution)/shard_map/dot_general | solution.py:176
  13.3 0.1 copy.67
  13.4 0.1 multiply_cosine_fusion
  13.7 1.0 maximum_maximum_fusion
  14.8 2.4 pad_maximum_fusion
  17.6 0.3 copy.64
  18.0 0.4 copy.65
  18.4 0.4 copy.66
  18.9 11.3 %reduce-window.6 = s32[40,8,128]{2,1,0:T(8,128)S(1)} reduce-window(s32[40,8,128]{2,1,0:T(8,128)S(1)} %fusion.17, s32[]{:T(128)} %constant.62.clone.1), window={size=1x1x128 pad=0_0x0_0x127_0}, to_apply=%region_1.0 | reduce-window | flops 5201920 | bytes 327684 | tf_op jit(solution)/shard_map/reduce-window
  30.3 0.1 copy.73
  30.9 0.7 pad_add_fusion.meta_ref
  31.6 1.4 pad_maximum_fusion.1
  33.0 1.6 fusion
  34.6 70.1 %all-gather.6.cloned.1.call-done = bf16[6144,1024]{1,0:T(8,128)(2,1)} async-done(((bf16[384,1024]{1,0:T(8,128)(2,1)}), bf16[6144,1024]{1,0:T(8,128)(2,1)}) %all-gather.6.cloned.1.call-update) | async-done | bytes 12582928 | tf_op jit(solution)/shard_map/all_gather | solution.py:187
  104.7 75.4 %shard_map.118 = bf16[8,384,64]{2,1,0:T(8,128)(2,1)} custom-call(s32[2]{0:T(128)} %pad_add_fusion.meta_ref, bf16[8,384,64]{2,1,0:T(8,128)(2,1)} %bitcast.56, bf16[16,384,1024]{2,1,0:T(8,128)(2,1)} %bitcast.51, bf16[16,384,1024]{2,1,0:T(8,128)(2,1)} %bitcast.52), custom_call_target="tpu_custom_call" | custom-call | tf_op jit(solution)/shard_map/pallas_call | solution.py:83
  180.1 1.4 copy.69
  181.5 3.5 %multiply_reduce_fusion = (f32[128]{0:T(128)S(1)}, f32[128,1536]{1,0:T(8,128)S(1)}) fusion(bf16[128,1536]{0,1:T(8,128)(2,1)S(1)} %bitcast.58, bf16[1536,1536]{1,0:T(8,128)(2,1)} %param.17, bf16[128,1536]{1,0:T(8,128)(2,1)S(1)} %copy-done.3), kind=kOutput, calls=%fused_computation.19 | convolution fusion | flops 605159296 | bytes 6291968 | tf_op jit(solution)/shard_map/dot_general | solution.py:195
  185.1 0.3 fusion.23
  185.7 0.2 copy.76
  185.9 3.4 %scatter_fusion = f32[1280,2]{1,0:T(8,128)S(1)} fusion(f32[1280,2]{1,0:T(8,128)S(1)} %copy-done.2, s32[1024]{0:T(1024)S(1)} %bitcast.66, f32[1024,2]{1,0:T(8,128)S(1)} %copy.76), kind=kCustom, calls=%fused_computation | custom fusion | bytes 28672 | tf_op jit(solution)/shard_map/scatter | solution.py:222
  189.3 0.9 copy.77
  190.2 10.3 %all-to-all-start = ((f32[8,160,2]{1,2,0:T(2,128)}), f32[8,160,2]{1,2,0:T(2,128)S(1)}, u32[]{:S(2)}, u32[]{:S(2)}) async-start(f32[8,160,2]{1,2,0:T(2,128)} %copy.77), calls=%async_computation | async-start | bytes 32768 | tf_op jit(solution)/shard_map/all_to_all | solution.py:224
  200.6 3.3 %convolution_convert_fusion = bf16[1280,1536]{1,0:T(8,128)(2,1)} fusion(pred[128,1280]{1,0:T(8,128)(4,1)S(1)} %fusion, f32[128,1536]{1,0:T(8,128)S(1)} %get-tuple-element.28, f32[1536]{0:T(1024)S(1)} %copy-done.6, f32[128]{0:T(128)S(1)} %add_rsqrt_fusion), kind=kOutput, calls=%fused_computation.1 | convolution fusion | flops 505872384 | bytes 4889088 | tf_op jit(solution)/shard_map/ts,td->sd/dot_general | solution.py:215
  203.8 2.1 all-to-all-done
  205.9 4.6 %all-to-all-start.1 = ((bf16[8,5,32,1536]{3,2,1,0:T(8,128)(2,1)}), bf16[8,5,32,1536]{3,2,1,0:T(8,128)(2,1)}, u32[]{:S(2)}, u32[]{:S(2)}) async-start(bf16[8,5,32,1536]{3,2,1,0:T(8,128)(2,1)} %bitcast.54), calls=%async_computation.1 | async-start | bytes 7864320 | tf_op jit(solution)/shard_map/all_to_all | solution.py:219
  210.6 46.8 %all-to-all-done.1.x_ref = bf16[8,5,32,1536]{3,2,1,0:T(8,128)(2,1)} async-done(((bf16[8,5,32,1536]{3,2,1,0:T(8,128)(2,1)}), bf16[8,5,32,1536]{3,2,1,0:T(8,128)(2,1)}, u32[]{:S(2)}, u32[]{:S(2)}) %all-to-all-start.1) | async-done | bytes 3932192 | tf_op jit(solution)/shard_map/all_to_all | solution.py:219
  257.4 12.5 %shard_map.119 = bf16[8,5,32,1536]{3,2,1,0:T(8,128)(2,1)S(1)} custom-call(bf16[8,5,32,1536]{3,2,1,0:T(8,128)(2,1)} %all-to-all-done.1.x_ref, bf16[5,512,4608]{2,1,0:T(8,128)(2,1)} %all-gather.4.cloned.1.call-done.w_ref), custom_call_target="tpu_custom_call" | custom-call | tf_op jit(solution)/shard_map/pallas_call | solution.py:123
  269.9 2.6 convolution_convert_fusion.1
  272.5 41.0 %all_to_all.15 = bf16[8,128,1536]{2,1,0:T(8,128)(2,1)S(1)} all-to-all(bf16[8,128,1536]{2,1,0:T(8,128)(2,1)S(1)} %convolution_convert_fusion.1), channel_id=1, replica_groups=mesh['req'=8,'shard'=16] {'req'}, dimensions={0} | all-to-all | bytes 6291456 | tf_op jit(solution)/shard_map/all_to_all | solution.py:237
  313.5 0.4 convert_reduce_fusion
  314.0 0.9 add_convert_fusion
  (57 shorter events, 1.8 us)
Async XLA Ops:
  6.5 178.5 %copy-start = (bf16[1536,40]{0,1:T(8,128)(2,1)S(1)}, bf16[1536,40]{0,1:T(8,128)(2,1)}, u32[]{:S(2)}) copy-start(bf16[1536,40]{0,1:T(8,128)(2,1)} %param.21) | copy-start | bytes 368644
  6.5 98.1 %all-gather.6.cloned.1.call-start = ((), (), s32[]{:S(2)}) async-start(), calls=%async_computation.4 | async-start | bytes 13369344 | tf_op jit(solution)/shard_map/all_gather | solution.py:187
  7.8 6.0 %copy-start.4 = (bf16[1,256,1024]{2,1,0:T(8,128)(2,1)S(1)}, bf16[1,256,1024]{2,1,0:T(8,128)(2,1)}, u32[]{:S(2)}) copy-start(bf16[1,256,1024]{2,1,0:T(8,128)(2,1)} %param.18) | copy-start | bytes 1572868
  12.5 2.3 copy-start.5
  14.7 2.6 copy-start.7
  14.8 242.6 %all-gather.4.cloned.1.call-start = ((), (), s32[]{:S(2)}) async-start(), calls=%async_computation.3 | async-start | bytes 25067520 | tf_op jit(solution)/shard_map/all_gather | solution.py:226
  104.7 76.8 %copy-start.3 = (bf16[128,1536]{1,0:T(8,128)(2,1)S(1)}, bf16[128,1536]{1,0:T(8,128)(2,1)}, u32[]{:S(2)}) copy-start(bf16[128,1536]{1,0:T(8,128)(2,1)} %param.14) | copy-start | bytes 1179652
  181.5 3.5 %copy-start.6 = (f32[1536]{0:T(1024)S(1)}, f32[1536]{0:T(1024)}, u32[]{:S(2)}) copy-start(f32[1536]{0:T(1024)} %param.20) | copy-start | bytes 18436
  181.5 4.4 %copy-start.2 = (f32[1280,2]{1,0:T(8,128)S(1)}, f32[1280,2]{1,0:T(8,128)}, u32[]{:S(2)}) copy-start(f32[1280,2]{1,0:T(8,128)} %constant.60.clone.1) | copy-start | bytes 30724
  190.2 15.7 %all-to-all-start = ((f32[8,160,2]{1,2,0:T(2,128)}), f32[8,160,2]{1,2,0:T(2,128)S(1)}, u32[]{:S(2)}, u32[]{:S(2)}) async-start(f32[8,160,2]{1,2,0:T(2,128)} %copy.77), calls=%async_computation | async-start | bytes 32768 | tf_op jit(solution)/shard_map/all_to_all | solution.py:224
  205.9 51.4 %all-to-all-start.1 = ((bf16[8,5,32,1536]{3,2,1,0:T(8,128)(2,1)}), bf16[8,5,32,1536]{3,2,1,0:T(8,128)(2,1)}, u32[]{:S(2)}, u32[]{:S(2)}) async-start(bf16[8,5,32,1536]{3,2,1,0:T(8,128)(2,1)} %bitcast.54), calls=%async_computation.1 | async-start | bytes 7864320 | tf_op jit(solution)/shard_map/all_to_all | solution.py:219
  272.5 42.3 %copy-start.1 = (bf16[1536,40]{0,1:T(8,128)(2,1)S(1)}, bf16[1536,40]{0,1:T(8,128)(2,1)}, u32[]{:S(2)}) copy-start(bf16[1536,40]{0,1:T(8,128)(2,1)} %param.21) | copy-start | bytes 368644
Sparse Core Ops, SparseCore 0:
  14.9 89.7 all-gather.5
  106.8 145.6 all-gather.3

commit v3 on v0

--- a/solution.py
+++ b/solution.py
@@ -204,7 +204,13 @@
     chosen = jnp.sum(jnp.where(picked, logits[:, None, :], 0.0), axis=-1)
     gates = jax.nn.softmax(chosen, axis=-1)
     flat_hot = picked.reshape(tok_rows * TOP, expert_count).astype(jnp.int32)
-    ranks = jnp.cumsum(flat_hot, axis=0) - flat_hot
+    pairs = flat_hot.shape[0]
+    before = (
+        lax.broadcasted_iota(jnp.int32, (pairs, pairs), 1)
+        < lax.broadcasted_iota(jnp.int32, (pairs, pairs), 0) + 0 * shard_pos
+    ).astype(jnp.bfloat16)
+    ranks = jnp.dot(before, flat_hot.astype(jnp.bfloat16), preferred_element_type=jnp.float32)
+    ranks = ranks.astype(jnp.int32)
     slot_rank = jnp.sum(ranks * flat_hot, axis=-1)
     slots = expert_ids.reshape(-1) * capacity + slot_rank
     slot_table = (

time: 325 us -> 325 us (level)
  other arithmetic: 21.5 us -> 10 us
  waiting for transfers between devices: 119 us -> 130 us
    another operation x5 -> x2, other arithmetic: 11.6 us -> 0.15 us
    all_gather x1, waiting for transfers between devices: 70.1 us -> 81.4 us  [local(): kv_all = lax.all_gather(joined, 'shard', axis=0, tiled=False)]
  transfers between devices with their start and end apart: 4 -> 4, of which waited for: 3 -> 3; matrix products, arithmetic and copies ran while one was open for 10% -> 7% of each run, Pallas kernels for 13% -> 13%
where the time goes in v3:
time: 325 us; the launch traced here: 323 us
  waiting for transfers between devices  130 us (40%)
  Pallas kernels  53.8 us (17%)
  starting transfers between devices  49.4 us (15%)
  blocking collectives  41 us (13%)
  matrix products  15.6 us (5%)
  between operations  14.4 us (4%)
  other arithmetic  10 us (3%)
  local copies, waits for them, and re-layouts  8.06 us (2%)
    all_gather x1, waiting for transfers between devices, local(): kv_all = lax.all_gather(joined, 'shard', axis=0, tiled=False)  81.4 us
    all_to_all x1, waiting for transfers between devices, local(): lax.all_to_all(outgoing, 'req', split_axis=0, concat_axis=0, tiled=True)  46.8 us
    all_to_all x1, starting transfers between devices, local(): tags = lax.all_to_all(tags, 'req', split_axis=0, concat_axis=0, tiled=True)  44.8 us
    pallas_call x1, Pallas kernels, attention(): pl.pallas_call(kern, out_shape=jax.ShapeDtypeStruct((KVH, rows, HD), jnp....  41.3 us
    all_to_all x1, blocking collectives, local(): lax.all_to_all(partial.astype(jnp.bfloat16), 'req', split_axis=0, concat_...  41 us
    pallas_call x1, Pallas kernels, experts(): pl.pallas_call(ffn_kernel, out_shape=jax.ShapeDtypeStruct(arrived.shape,...  12.5 us
  transfers between devices with their start and end apart: 4, of which 3 were waited for; matrix products, arithmetic and copies ran while one was open for 7% of the time, Pallas kernels for 13%

profile of v3, /device:TPU:30, one launch (start us, length us, event | category | flops | bytes accessed | tf_op | source)
XLA Modules:
  0.0 322.7 jit_solution(16179512431054505823)
XLA Ops:
  6.6 1.2 fusion.7
  7.8 4.7 %fusion.11 = f32[128,2560]{1,0:T(8,128)S(1)} fusion(bf16[1536,2560]{1,0:T(8,128)(2,1)} %param.16, bf16[128,1536]{1,0:T(8,128)(2,1)} %param.14, f32[1536]{0:T(1024)} %param.15, f32[128]{0:T(128)S(1)} %add_rsqrt_fusion.1), kind=kOutput, calls=%fused_computation.27 | convolution fusion | flops 1007419392 | bytes 9574912 | tf_op jit(solution)/shard_map/dot_general | solution.py:176
  13.3 0.1 copy.58
  13.4 0.1 multiply_cosine_fusion
  13.6 0.1 copy.59
  13.7 1.0 maximum_maximum_fusion
  14.8 2.4 pad_maximum_fusion
  17.3 0.3 copy.55
  17.7 0.4 copy.56
  18.1 0.4 copy.57
  18.8 0.6 fusion.6
  19.6 0.7 pad_add_fusion.meta_ref
  20.2 1.4 pad_maximum_fusion.1
  21.6 1.6 fusion
  23.3 81.4 %all-gather.6.cloned.1.call-done = bf16[6144,1024]{1,0:T(8,128)(2,1)} async-done(((bf16[384,1024]{1,0:T(8,128)(2,1)}), bf16[6144,1024]{1,0:T(8,128)(2,1)}) %all-gather.6.cloned.1.call-update) | async-done | bytes 12582928 | tf_op jit(solution)/shard_map/all_gather | solution.py:187
  104.7 41.3 %shard_map.118 = bf16[8,384,64]{2,1,0:T(8,128)(2,1)} custom-call(s32[2]{0:T(128)} %pad_add_fusion.meta_ref, bf16[8,384,64]{2,1,0:T(8,128)(2,1)} %bitcast.38, bf16[16,384,1024]{2,1,0:T(8,128)(2,1)} %bitcast.33, bf16[16,384,1024]{2,1,0:T(8,128)(2,1)} %bitcast.34), custom_call_target="tpu_custom_call" | custom-call | tf_op jit(solution)/shard_map/pallas_call | solution.py:83
  146.0 1.4 copy.60
  147.4 3.3 %multiply_reduce_fusion = (f32[128]{0:T(128)S(1)}, f32[128,1536]{1,0:T(8,128)S(1)}) fusion(bf16[128,1536]{0,1:T(8,128)(2,1)S(1)} %bitcast.40, bf16[1536,1536]{1,0:T(8,128)(2,1)} %param.17, bf16[128,1536]{1,0:T(8,128)(2,1)S(1)} %copy-done.3), kind=kOutput, calls=%fused_computation.24 | convolution fusion | flops 605159296 | bytes 6291968 | tf_op jit(solution)/shard_map/dot_general | solution.py:195
  150.8 0.3 fusion.24
  151.4 0.2 copy.64
  151.6 3.4 %scatter_fusion = f32[1280,2]{1,0:T(8,128)S(1)} fusion(f32[1280,2]{1,0:T(8,128)S(1)} %copy-done.2, s32[1024]{0:T(1024)S(1)} %bitcast.46, f32[1024,2]{1,0:T(8,128)S(1)} %copy.64), kind=kCustom, calls=%fused_computation | custom fusion | bytes 28672 | tf_op jit(solution)/shard_map/scatter | solution.py:228
  155.0 0.9 copy.65
  155.9 44.8 %all-to-all-start = ((f32[8,160,2]{1,2,0:T(2,128)}), f32[8,160,2]{1,2,0:T(2,128)S(1)}, u32[]{:S(2)}, u32[]{:S(2)}) async-start(f32[8,160,2]{1,2,0:T(2,128)} %copy.65), calls=%async_computation | async-start | bytes 32768 | tf_op jit(solution)/shard_map/all_to_all | solution.py:230
  200.8 3.3 %convolution_convert_fusion = bf16[1280,1536]{1,0:T(8,128)(2,1)} fusion(pred[128,1280]{1,0:T(8,128)(4,1)S(1)} %fusion, f32[128,1536]{1,0:T(8,128)S(1)} %get-tuple-element.28, f32[1536]{0:T(1024)S(1)} %copy-done.6, f32[128]{0:T(128)S(1)} %add_rsqrt_fusion), kind=kOutput, calls=%fused_computation.1 | convolution fusion | flops 505872384 | bytes 4889088 | tf_op jit(solution)/shard_map/ts,td->sd/dot_general | solution.py:221
  204.0 2.1 all-to-all-done
  206.1 4.6 %all-to-all-start.1 = ((bf16[8,5,32,1536]{3,2,1,0:T(8,128)(2,1)}), bf16[8,5,32,1536]{3,2,1,0:T(8,128)(2,1)}, u32[]{:S(2)}, u32[]{:S(2)}) async-start(bf16[8,5,32,1536]{3,2,1,0:T(8,128)(2,1)} %bitcast.36), calls=%async_computation.1 | async-start | bytes 7864320 | tf_op jit(solution)/shard_map/all_to_all | solution.py:225
  210.7 46.8 %all-to-all-done.1.x_ref = bf16[8,5,32,1536]{3,2,1,0:T(8,128)(2,1)} async-done(((bf16[8,5,32,1536]{3,2,1,0:T(8,128)(2,1)}), bf16[8,5,32,1536]{3,2,1,0:T(8,128)(2,1)}, u32[]{:S(2)}, u32[]{:S(2)}) %all-to-all-start.1) | async-done | bytes 3932192 | tf_op jit(solution)/shard_map/all_to_all | solution.py:225
  257.5 12.5 %shard_map.119 = bf16[8,5,32,1536]{3,2,1,0:T(8,128)(2,1)S(1)} custom-call(bf16[8,5,32,1536]{3,2,1,0:T(8,128)(2,1)} %all-to-all-done.1.x_ref, bf16[5,512,4608]{2,1,0:T(8,128)(2,1)} %all-gather.4.cloned.1.call-done.w_ref), custom_call_target="tpu_custom_call" | custom-call | tf_op jit(solution)/shard_map/pallas_call | solution.py:123
  270.1 3.5 %convolution_convert_fusion.1 = bf16[8,128,1536]{2,1,0:T(8,128)(2,1)S(1)} fusion(bf16[8,160,1536]{2,1,0:T(8,128)(2,1)S(1)} %bitcast.32, f32[8,160]{1,0:T(8,128)S(1)} %get-tuple-element.29, s32[8,160]{1,0:T(8,128)S(1)} %get-tuple-element.30), kind=kOutput, calls=%fused_computation.7 | convolution fusion | flops 3021799424 | bytes 7088128 | tf_op jit(solution)/shard_map/stm,smd->std/dot_general | solution.py:239
  273.5 41.0 %all_to_all.15 = bf16[8,128,1536]{2,1,0:T(8,128)(2,1)S(1)} all-to-all(bf16[8,128,1536]{2,1,0:T(8,128)(2,1)S(1)} %convolution_convert_fusion.1), channel_id=1, replica_groups=mesh['req'=8,'shard'=16] {'req'}, dimensions={0} | all-to-all | bytes 6291456 | tf_op jit(solution)/shard_map/all_to_all | solution.py:243
  314.6 0.4 convert_reduce_fusion
  315.0 0.9 add_convert_fusion
  (48 shorter events, 1.3 us)
Async XLA Ops:
  6.5 144.2 %copy-start = (bf16[1536,40]{0,1:T(8,128)(2,1)S(1)}, bf16[1536,40]{0,1:T(8,128)(2,1)}, u32[]{:S(2)}) copy-start(bf16[1536,40]{0,1:T(8,128)(2,1)} %param.21) | copy-start | bytes 368644
  6.5 98.1 %all-gather.6.cloned.1.call-start = ((), (), s32[]{:S(2)}) async-start(), calls=%async_computation.4 | async-start | bytes 13369344 | tf_op jit(solution)/shard_map/all_gather | solution.py:187
  7.8 6.0 %copy-start.4 = (bf16[1,256,1024]{2,1,0:T(8,128)(2,1)S(1)}, bf16[1,256,1024]{2,1,0:T(8,128)(2,1)}, u32[]{:S(2)}) copy-start(bf16[1,256,1024]{2,1,0:T(8,128)(2,1)} %param.18) | copy-start | bytes 1572868
  12.5 2.3 copy-start.5
  14.7 242.8 %all-gather.4.cloned.1.call-start = ((), (), s32[]{:S(2)}) async-start(), calls=%async_computation.3 | async-start | bytes 25067520 | tf_op jit(solution)/shard_map/all_gather | solution.py:232
  17.2 1.4 copy-start.7
  104.7 42.7 %copy-start.3 = (bf16[128,1536]{1,0:T(8,128)(2,1)S(1)}, bf16[128,1536]{1,0:T(8,128)(2,1)}, u32[]{:S(2)}) copy-start(bf16[128,1536]{1,0:T(8,128)(2,1)} %param.14) | copy-start | bytes 1179652
  147.4 3.3 %copy-start.6 = (f32[1536]{0:T(1024)S(1)}, f32[1536]{0:T(1024)}, u32[]{:S(2)}) copy-start(f32[1536]{0:T(1024)} %param.20) | copy-start | bytes 18436
  147.4 4.2 %copy-start.2 = (f32[1280,2]{1,0:T(8,128)S(1)}, f32[1280,2]{1,0:T(8,128)}, u32[]{:S(2)}) copy-start(f32[1280,2]{1,0:T(8,128)} %constant.57.clone.1) | copy-start | bytes 30724
  155.9 50.2 %all-to-all-start = ((f32[8,160,2]{1,2,0:T(2,128)}), f32[8,160,2]{1,2,0:T(2,128)S(1)}, u32[]{:S(2)}, u32[]{:S(2)}) async-start(f32[8,160,2]{1,2,0:T(2,128)} %copy.65), calls=%async_computation | async-start | bytes 32768 | tf_op jit(solution)/shard_map/all_to_all | solution.py:230
  206.1 51.4 %all-to-all-start.1 = ((bf16[8,5,32,1536]{3,2,1,0:T(8,128)(2,1)}), bf16[8,5,32,1536]{3,2,1,0:T(8,128)(2,1)}, u32[]{:S(2)}, u32[]{:S(2)}) async-start(bf16[8,5,32,1536]{3,2,1,0:T(8,128)(2,1)} %bitcast.36), calls=%async_computation.1 | async-start | bytes 7864320 | tf_op jit(solution)/shard_map/all_to_all | solution.py:225
  273.5 42.3 %copy-start.1 = (bf16[1536,40]{0,1:T(8,128)(2,1)S(1)}, bf16[1536,40]{0,1:T(8,128)(2,1)}, u32[]{:S(2)}) copy-start(bf16[1536,40]{0,1:T(8,128)(2,1)} %param.21) | copy-start | bytes 368644
Sparse Core Ops, SparseCore 0:
  14.9 89.7 all-gather.5
  106.8 145.6 all-gather.3
